TPU v7x, 512 devices: a whole 4x4x16 slice. The times are simulated.
512 devices in a mesh: ctx: 64 (over z, x_lo, core), tp: 8 (over y, x_hi).
Axes of the slice: x: 4 (x_hi: 2, x_lo: 2; x = x_hi * 2 + x_lo), y: 4, z: 16, core: 2. Of those that a mesh axis runs over, the one named last changes fastest.
Arguments:
- queries: bfloat16 [8192, 4096], P('ctx', 'tp'), may hold values from -5 to 5
- keys: bfloat16 [8192, 1024], P('ctx', 'tp'), may hold values from -5 to 5
- values: bfloat16 [8192, 1024], P('ctx', 'tp'), may hold values from -6 to 6
- docs: int32 [8192], P('ctx'), may hold values from 0 to 11, never falling along the last dimension, each value on 1 to 4224 neighbouring positions
- out_weight: bfloat16 [4096, 4096], P('tp'), may hold values from -0.09375 to 0.09375
Outputs:
- mixed: bfloat16 [8192, 4096], P('ctx', 'tp')
All inputs are finite; a program needn't handle non-finite values.
Results may differ from a plain program's by a relative error of at most 0.014.
Values may be sent and summed in bfloat16 or wider, within the bound.
No kernel may reach another device: no remote copies, remote signals or barrier semaphores. Data moves between devices by JAX's collectives and lax.ppermute only.
A program may use at most 64 MiB of HBM per device.

v0:
```python
import math
import jax
import jax.numpy as jnp
from jax import lax
from jax.sharding import PartitionSpec as P

HEAD_DIM = 128
neg_large = -1e30


def attend(state, query_half, query_pos, query_doc, key_part, value_part, key_pos, key_doc):
    peak, total, accum = state
    scores = jnp.einsum("igkd,jgd->gkij", query_half, key_part, preferred_element_type=jnp.float32)
    scores = scores * (1.0 / math.sqrt(key_part.shape[-1]))
    allowed = (key_pos[None, :] <= query_pos[:, None]) & (key_doc[None, :] == query_doc[:, None])
    block_peak = jnp.max(jnp.where(allowed, scores, neg_large), axis=-1)
    new_peak = jnp.maximum(peak, block_peak)
    rescale = jnp.exp(peak - new_peak)
    weights = jnp.where(allowed, jnp.exp(scores - new_peak[..., None]), 0.0)
    total = total * rescale + jnp.sum(weights, axis=-1)
    update = jnp.einsum(
        "gkij,jgd->gkid",
        weights.astype(jnp.bfloat16),
        value_part,
        preferred_element_type=jnp.float32,
    )
    accum = accum * rescale[..., None] + update
    return (new_peak, total, accum)


def visit(state, query_half, query_pos, query_doc, key_part, value_part, key_pos, key_doc):
    needed = jnp.min(key_pos) <= jnp.max(query_pos)

    def compute(current):
        return attend(
            current, query_half, query_pos, query_doc, key_part, value_part, key_pos, key_doc
        )

    def unchanged(current):
        return current

    return lax.cond(needed, compute, unchanged, state)


def finish(state):
    peak, total, accum = state
    summed = accum / total[..., None]
    kv_count, group_size, row_count, head_dim = summed.shape
    summed = jnp.transpose(summed, (2, 0, 1, 3)).reshape(
        row_count, kv_count * group_size * head_dim
    )
    return summed.astype(jnp.bfloat16)


def shards(queries, keys, values, docs, out_weight):
    row_count = queries.shape[0]
    half_rows = row_count // 2
    head_dim = HEAD_DIM
    kv_local = keys.shape[1] // head_dim
    group_size = queries.shape[1] // keys.shape[1]
    my_index = lax.axis_index("ctx")
    all_docs = lax.all_gather(docs, "ctx", axis=0, tiled=True)
    offsets = jnp.arange(half_rows, dtype=jnp.int32)
    shard_offsets = jnp.arange(row_count, dtype=jnp.int32)
    lower_queries = queries[:half_rows]
    upper_queries = queries[half_rows:]
    low_positions = my_index * row_count + offsets
    high_positions = my_index * row_count + half_rows + offsets
    low_docs = jnp.take(all_docs, low_positions)
    high_docs = jnp.take(all_docs, high_positions)
    query_low = lower_queries.reshape(half_rows, kv_local, group_size, head_dim)
    query_high = upper_queries.reshape(half_rows, kv_local, group_size, head_dim)
    empty = (
        jnp.full((kv_local, group_size, half_rows), neg_large, jnp.float32),
        jnp.zeros((kv_local, group_size, half_rows), jnp.float32),
        jnp.zeros((kv_local, group_size, half_rows, head_dim), jnp.float32),
    )
    carry = (empty, empty)
    key_piece = lax.all_gather(keys, "ctx", axis=0, tiled=True)
    value_piece = lax.all_gather(values, "ctx", axis=0, tiled=True)
    shard_count = key_piece.shape[0] // row_count
    shaped_keys = key_piece.reshape(shard_count, row_count, kv_local, head_dim)
    shaped_values = value_piece.reshape(shard_count, row_count, kv_local, head_dim)
    shard_numbers = jnp.arange(shard_count, dtype=jnp.int32)

    def one_shard(states, inputs):
        key_part, value_part, shard_number = inputs
        key_pos = shard_number * row_count + shard_offsets
        key_doc = jnp.take(all_docs, key_pos)
        state_low, state_high = states
        state_low = visit(
            state_low, query_low, low_positions, low_docs, key_part, value_part, key_pos, key_doc
        )
        state_high = visit(
            state_high,
            query_high,
            high_positions,
            high_docs,
            key_part,
            value_part,
            key_pos,
            key_doc,
        )
        return ((state_low, state_high), None)

    carry, unused = lax.scan(one_shard, carry, (shaped_keys, shaped_values, shard_numbers))
    attention = jnp.concatenate([finish(carry[0]), finish(carry[1])], axis=0)
    partial_terms = jnp.dot(attention, out_weight, preferred_element_type=jnp.float32)
    mixed = lax.psum_scatter(
        partial_terms.astype(jnp.bfloat16), "tp", scatter_dimension=1, tiled=True
    )
    return mixed


def solution(mesh):
    placed = (P("ctx", "tp"), P("ctx", "tp"), P("ctx", "tp"), P("ctx"), P("tp", None))
    return jax.shard_map(
        shards, mesh=mesh, in_specs=placed, out_specs=P("ctx", "tp"), check_vma=False
    )
```

profile of v0, /device:TPU:32, one launch (start us, length us, event | category | flops | bytes accessed | tf_op | source)
XLA Modules:
  0.0 863.5 jit_solution(10624895469857638994)
XLA Ops:
  8.1 66.9 %all-gather = s32[64,1,128]{2,1,0:T(1,128)S(1)} all-gather(s32[1,1,128]{2,1,0:T(1,128)} %bitcast.123), channel_id=1, replica_groups=mesh['ctx'=64,'tp'=8] {'ctx'}, dimensions={0}, use_global_device_ids=true | all-gather | bytes 33280 | tf_op jit(solution)/shard_map/all_gather | solution.py:62
  78.2 57.6 %all-gather.4.cloned.1.call-done = bf16[8192,128]{1,0:T(8,128)(2,1)} async-done(((bf16[128,128]{1,0:T(8,128)(2,1)}), bf16[8192,128]{1,0:T(8,128)(2,1)}) %all-gather.4.cloned.1.call-update) | async-done | bytes 2097168 | tf_op jit(solution)/shard_map/all_gather | solution.py:79
  135.9 120.6 %all-gather.6.cloned.1.call-done = bf16[8192,128]{1,0:T(8,128)(2,1)} async-done(((bf16[128,128]{1,0:T(8,128)(2,1)}), bf16[8192,128]{1,0:T(8,128)(2,1)}) %all-gather.6.cloned.1.call-update) | async-done | bytes 2097168 | tf_op jit(solution)/shard_map/all_gather | solution.py:80
  256.6 417.2 %while.22 = (s32[]{:T(128)}, f32[1,4,64]{2,1,0:T(4,128)S(1)}, f32[1,4,64]{2,1,0:T(4,128)S(1)}, f32[1,4,64,128]{3,2,1,0:T(8,128)S(1)}, f32[1,4,64]{2,1,0:T(4,128)...) while((s32[]{:T(128)}, f32[1,4,64]{2,1,0:T(4,128)S(1)}, ...), condition=%wide.region_12.14_spmd.clone, body=%wide.region_2.13_spmd.clone.sunk | while | flops 34328964 | bytes 1815597 | solution.py:106
  257.8 1.1 gather_fusion
  265.9 1.1 gather_fusion
  274.0 1.1 gather_fusion
  282.1 1.1 gather_fusion
  290.2 1.1 gather_fusion
  298.2 1.1 gather_fusion
  304.6 1.1 gather_fusion
  311.0 1.1 gather_fusion
  317.4 1.1 gather_fusion
  323.8 1.1 gather_fusion
  330.2 1.1 gather_fusion
  336.6 1.1 gather_fusion
  342.9 1.1 gather_fusion
  349.3 1.1 gather_fusion
  355.7 1.1 gather_fusion
  362.1 1.1 gather_fusion
  368.5 1.1 gather_fusion
  374.9 1.1 gather_fusion
  381.3 1.1 gather_fusion
  387.6 1.1 gather_fusion
  394.0 1.1 gather_fusion
  400.4 1.1 gather_fusion
  406.8 1.1 gather_fusion
  413.2 1.1 gather_fusion
  419.6 1.1 gather_fusion
  426.0 1.1 gather_fusion
  432.3 1.1 gather_fusion
  438.7 1.1 gather_fusion
  445.1 1.1 gather_fusion
  451.5 1.1 gather_fusion
  457.9 1.1 gather_fusion
  464.3 1.1 gather_fusion
  470.7 1.1 gather_fusion
  477.0 1.1 gather_fusion
  483.4 1.1 gather_fusion
  489.8 1.1 gather_fusion
  496.2 1.1 gather_fusion
  502.6 1.1 gather_fusion
  509.0 1.1 gather_fusion
  515.4 1.1 gather_fusion
  521.7 1.1 gather_fusion
  528.1 1.1 gather_fusion
  534.5 1.1 gather_fusion
  540.9 1.1 gather_fusion
  547.3 1.1 gather_fusion
  553.7 1.1 gather_fusion
  560.1 1.1 gather_fusion
  566.4 1.1 gather_fusion
  572.8 1.1 gather_fusion
  579.2 1.1 gather_fusion
  585.6 1.1 gather_fusion
  592.0 1.1 gather_fusion
  598.4 1.1 gather_fusion
  604.8 1.1 gather_fusion
  611.1 1.1 gather_fusion
  617.5 1.1 gather_fusion
  623.9 1.1 gather_fusion
  630.3 1.1 gather_fusion
  674.1 3.9 convolution_convert_fusion
  678.1 178.9 %reduce-scatter.2.cloned.1.call-done = bf16[128,512]{1,0:T(8,128)(2,1)} async-done(((bf16[128,4096]{1,0:T(8,128)(2,1)}), bf16[128,512]{1,0:T(8,128)(2,1)}) %reduce-scatter.2.cloned.1.call-update) | async-done | bytes 131088 | tf_op jit(solution)/shard_map/reduce_scatter | solution.py:109
  (758 shorter events, 162.4 us)
Async XLA Ops:
  6.5 129.3 %all-gather.4.cloned.1.call-start = ((), (), s32[]{:S(2)}) async-start(), calls=%async_computation.1 | async-start | bytes 2129920 | tf_op jit(solution)/shard_map/all_gather | solution.py:79
  7.3 249.2 %all-gather.6.cloned.1.call-start = ((), (), s32[]{:S(2)}) async-start(), calls=%async_computation.2 | async-start | bytes 2129920 | tf_op jit(solution)/shard_map/all_gather | solution.py:80
  8.0 849.0 %reduce-scatter.2.cloned.1.call-start = ((), (), s32[]{:S(2)}) async-start(), calls=%async_computation.3 | async-start | bytes 1179648 | tf_op jit(solution)/shard_map/reduce_scatter | solution.py:109
Sparse Core Ops, SparseCore 0:
  9.5 126.3 all-gather.3
  138.0 118.4 all-gather.5
  678.2 178.6 reduce-scatter.1
where the time goes:
time: 871 us; the launch traced here: 863 us
  waiting for transfers between devices  359 us (41%)
  loops' own time  203 us (23%)
  local copies, waits for them, and re-layouts  165 us (19%)
  blocking collectives  66.9 us (8%)
  other arithmetic  47.5 us (5%)
  between operations  13.2 us (2%)
  matrix products  9.02 us (1%)
    another operation x1, loops' own time, shards(): lax.scan(one_shard, carry, (shaped_keys, shaped_values, shard_numbers))  201 us
    reduce_scatter x1, waiting for transfers between devices, shards(): lax.psum_scatter(partial_terms.astype(jnp.bfloat16), 'tp', scatter_dimens...  179 us
    all_gather x1, waiting for transfers between devices, shards(): value_piece = lax.all_gather(values, 'ctx', axis=0, tiled=True)  121 us
    gather x64, local copies, waits for them, and re-layouts, one_shard(): key_doc = jnp.take(all_docs, key_pos)  73.5 us
    all_gather x1, blocking collectives, shards(): all_docs = lax.all_gather(docs, 'ctx', axis=0, tiled=True)  66.9 us
    all_gather x1, waiting for transfers between devices, shards(): key_piece = lax.all_gather(keys, 'ctx', axis=0, tiled=True)  57.6 us
    squeeze x64, local copies, waits for them, and re-layouts, shards(): lax.scan(one_shard, carry, (shaped_keys, shaped_values, shard_numbers))  50.4 us
    reduce_min x64, other arithmetic, visit(): needed = jnp.min(key_pos) <= jnp.max(query_pos)  42.4 us
  transfers between devices with their start and end apart: 3, of which 3 were waited for; matrix products, arithmetic and copies ran while one was open for 0% of the time, Pallas kernels for 0%

commit v1 on v0

--- a/solution.py
+++ b/solution.py
@@ -76,8 +76,11 @@
         jnp.zeros((kv_local, group_size, half_rows, head_dim), jnp.float32),
     )
     carry = (empty, empty)
-    key_piece = lax.all_gather(keys, "ctx", axis=0, tiled=True)
-    value_piece = lax.all_gather(values, "ctx", axis=0, tiled=True)
+    key_piece, value_piece = jnp.split(
+        lax.all_gather(jnp.concatenate([keys, values], axis=1), "ctx", axis=0, tiled=True),
+        [keys.shape[1]],
+        axis=1,
+    )
     shard_count = key_piece.shape[0] // row_count
     shaped_keys = key_piece.reshape(shard_count, row_count, kv_local, head_dim)
     shaped_values = value_piece.reshape(shard_count, row_count, kv_local, head_dim)

time: 871 us -> 774 us (0.89)
  waiting for transfers between devices: 359 us -> 238 us
  loops' own time: 203 us -> 218 us
    all_gather x2 -> x1, waiting for transfers between devices: 178 us -> 59.4 us  [shards(): lax.all_gather(jnp.concatenate([keys, values], axis=1), 'ctx', axis=0, ti...]
    another operation x1, loops' own time: 201 us -> 216 us  [shards(): lax.scan(one_shard, carry, (shaped_keys, shaped_values, shard_numbers))]
  transfers between devices with their start and end apart: 3 -> 2, of which waited for: 3 -> 2; matrix products, arithmetic and copies ran while one was open for 0% -> 1% of each run, Pallas kernels for 0% -> 0%
where the time goes in v1:
time: 774 us; the launch traced here: 766 us
  waiting for transfers between devices  238 us (31%)
  loops' own time  218 us (28%)
  local copies, waits for them, and re-layouts  167 us (22%)
  blocking collectives  66.9 us (9%)
  other arithmetic  52.7 us (7%)
  between operations  13.5 us (2%)
  matrix products  9.04 us (1%)
    another operation x1, loops' own time, shards(): lax.scan(one_shard, carry, (shaped_keys, shaped_values, shard_numbers))  216 us
    reduce_scatter x1, waiting for transfers between devices, shards(): lax.psum_scatter(partial_terms.astype(jnp.bfloat16), 'tp', scatter_dimens...  179 us
    gather x64, local copies, waits for them, and re-layouts, one_shard(): key_doc = jnp.take(all_docs, key_pos)  73.5 us
    all_gather x1, blocking collectives, shards(): all_docs = lax.all_gather(docs, 'ctx', axis=0, tiled=True)  66.9 us
    all_gather x1, waiting for transfers between devices, shards(): lax.all_gather(jnp.concatenate([keys, values], axis=1), 'ctx', axis=0, ti...  59.4 us
    squeeze x64, local copies, waits for them, and re-layouts, shards(): lax.scan(one_shard, carry, (shaped_keys, shaped_values, shard_numbers))  49.3 us
    reduce_min x64, other arithmetic, visit(): needed = jnp.min(key_pos) <= jnp.max(query_pos)  45.5 us
    dynamic_slice x64, local copies, waits for them, and re-layouts, shards(): lax.scan(one_shard, carry, (shaped_keys, shaped_values, shard_numbers))  37.6 us
  transfers between devices with their start and end apart: 2, of which 2 were waited for; matrix products, arithmetic and copies ran while one was open for 1% of the time, Pallas kernels for 0%

profile of v1, /device:TPU:32, one launch (start us, length us, event | category | flops | bytes accessed | tf_op | source)
XLA Modules:
  0.0 766.0 jit_solution(10819931098444831321)
XLA Ops:
  6.5 1.4 pad_maximum_fusion
  8.0 66.9 %all-gather = s32[64,1,128]{2,1,0:T(1,128)S(1)} all-gather(s32[1,1,128]{2,1,0:T(1,128)} %bitcast.123), channel_id=1, replica_groups=mesh['ctx'=64,'tp'=8] {'ctx'}, dimensions={0}, use_global_device_ids=true | all-gather | bytes 33280 | tf_op jit(solution)/shard_map/all_gather | solution.py:62
  78.8 59.4 %all-gather.3.cloned.1.call-done = bf16[8192,256]{1,0:T(8,128)(2,1)} async-done(((bf16[128,256]{1,0:T(8,128)(2,1)}), bf16[8192,256]{1,0:T(8,128)(2,1)}) %all-gather.3.cloned.1.call-update) | async-done | bytes 4194320 | tf_op jit(solution)/shard_map/all_gather | solution.py:80
  138.2 3.8 fusion.44
  142.1 433.7 %while.22 = (s32[]{:T(128)}, f32[1,4,64]{2,1,0:T(4,128)S(1)}, f32[1,4,64]{2,1,0:T(4,128)S(1)}, f32[1,4,64,128]{3,2,1,0:T(8,128)S(1)}, f32[1,4,64]{2,1,0:T(4,128)...) while((s32[]{:T(128)}, f32[1,4,64]{2,1,0:T(4,128)S(1)}, ...), condition=%wide.region_12.14_spmd.clone, body=%wide.region_2.13_spmd.clone.sunk | while | flops 34328964 | bytes 1815597 | solution.py:109
  143.4 1.1 gather_fusion
  151.7 1.1 gather_fusion
  160.0 1.1 gather_fusion
  168.4 1.1 gather_fusion
  176.7 1.1 gather_fusion
  185.1 1.1 gather_fusion
  191.7 1.1 gather_fusion
  198.4 1.1 gather_fusion
  205.0 1.1 gather_fusion
  211.7 1.1 gather_fusion
  218.3 1.1 gather_fusion
  224.9 1.1 gather_fusion
  231.6 1.1 gather_fusion
  238.2 1.1 gather_fusion
  244.9 1.1 gather_fusion
  251.5 1.1 gather_fusion
  258.2 1.1 gather_fusion
  264.8 1.1 gather_fusion
  271.5 1.1 gather_fusion
  278.1 1.1 gather_fusion
  284.7 1.1 gather_fusion
  291.4 1.1 gather_fusion
  298.0 1.1 gather_fusion
  304.7 1.1 gather_fusion
  311.3 1.1 gather_fusion
  318.0 1.1 gather_fusion
  324.6 1.1 gather_fusion
  331.2 1.1 gather_fusion
  337.9 1.1 gather_fusion
  344.5 1.1 gather_fusion
  351.2 1.1 gather_fusion
  357.8 1.1 gather_fusion
  364.5 1.1 gather_fusion
  371.1 1.1 gather_fusion
  377.8 1.1 gather_fusion
  384.4 1.1 gather_fusion
  391.0 1.1 gather_fusion
  397.7 1.1 gather_fusion
  404.3 1.1 gather_fusion
  411.0 1.1 gather_fusion
  417.6 1.1 gather_fusion
  424.3 1.1 gather_fusion
  430.9 1.1 gather_fusion
  437.6 1.1 gather_fusion
  444.2 1.1 gather_fusion
  450.8 1.1 gather_fusion
  457.5 1.1 gather_fusion
  464.1 1.1 gather_fusion
  470.8 1.1 gather_fusion
  477.4 1.1 gather_fusion
  484.1 1.1 gather_fusion
  490.7 1.1 gather_fusion
  497.4 1.1 gather_fusion
  504.0 1.1 gather_fusion
  510.6 1.1 gather_fusion
  517.3 1.1 gather_fusion
  523.9 1.1 gather_fusion
  576.2 4.0 convolution_convert_fusion
  580.2 179.0 %reduce-scatter.2.cloned.1.call-done = bf16[128,512]{1,0:T(8,128)(2,1)} async-done(((bf16[128,4096]{1,0:T(8,128)(2,1)}), bf16[128,512]{1,0:T(8,128)(2,1)}) %reduce-scatter.2.cloned.1.call-update) | async-done | bytes 131088 | tf_op jit(solution)/shard_map/reduce_scatter | solution.py:112
  (757 shorter events, 164.4 us)
Async XLA Ops:
  6.5 131.6 %all-gather.3.cloned.1.call-start = ((), (), s32[]{:S(2)}) async-start(), calls=%async_computation.1 | async-start | bytes 4259840 | tf_op jit(solution)/shard_map/all_gather | solution.py:80
  8.0 751.2 %reduce-scatter.2.cloned.1.call-start = ((), (), s32[]{:S(2)}) async-start(), calls=%async_computation.2 | async-start | bytes 1179648 | tf_op jit(solution)/shard_map/reduce_scatter | solution.py:112
Sparse Core Ops, SparseCore 0:
  9.5 128.6 all-gather.2
  580.3 178.8 reduce-scatter.1
